TPU v7x, 256 devices: a whole 4x4x8 slice. The times are simulated.
256 devices in a mesh: gx: 32 (over z_hi, y, core), gy: 8 (over z_lo, x).
Axes of the slice: x: 4, y: 4, z: 8 (z_hi: 4, z_lo: 2; z = z_hi * 2 + z_lo), core: 2. Of those that a mesh axis runs over, the one named last changes fastest.
Arguments:
- state: float32 [5, 256, 64, 128], P(None, 'gx', 'gy'), may hold values from -6 to 6
- terrain: int32 [256, 64], P('gx', 'gy'), may hold values from 0 to 31
- site_cells: int32 [65536], P(('gx', 'gy')), may hold values from 0 to 8191
- site_values: float32 [5, 65536], P(None, ('gx', 'gy')), may hold values from -6 to 6
- w_in: float32 [64, 4], replicated, may hold values from -3 to 3
- b_in: float32 [64], replicated, may hold values from -3 to 3
- w_out: float32 [64], replicated, may hold values from -1.5 to 1.5
Outputs:
- state_grad: float32 [5, 256, 64, 128], P(None, 'gx', 'gy')
- closure_grad: float32 [64, 6], replicated
Inputs may be any that keep to these rules, and one draw needn't show every extreme that they name: `site_cells`: site s lies on the device that holds entry s; its id names a cell of that device's block as (i * 8 + j) * 128 + k for local position (i, j, k).
All inputs are finite; a program needn't handle non-finite values.
Results may differ from a plain program's by a relative error of at most 0.0003.
Values sent between devices are 32-bit elements; how exact they have to be, the bound alone decides.
No kernel may reach another device: no remote copies, remote signals or barrier semaphores. Data moves between devices by JAX's collectives and lax.ppermute only.
A program may use at most 128 MiB of HBM per device.

v0:
```python
import jax
import jax.numpy as jnp
from jax import lax
from jax.sharding import PartitionSpec as P

STEPS = 4
PRECISE = lax.Precision.HIGHEST


def padded_2(cells, sides, width):
    for axis, dim in sides:
        count = lax.axis_size(axis)
        ends = count - 1
        head = lax.slice_in_dim(cells, 0, width, axis=dim)
        tail = lax.slice_in_dim(cells, cells.shape[dim] - width, cells.shape[dim], axis=dim)
        cells = jnp.concatenate(
            [
                lax.ppermute(tail, axis, [(i, (i + 1) % count) for i in range(ends)]),
                cells,
                lax.ppermute(head, axis, [((i + 1) % count, i) for i in range(ends)]),
            ],
            axis=dim,
        )
    return cells


def vertical_diff(values):
    blank = jnp.zeros_like(values[..., :1])
    upper = jnp.concatenate([values[..., 1:], blank], axis=-1)
    lower = jnp.concatenate([blank, values[..., :-1]], axis=-1)
    return 0.5 * (upper - lower)


def closure_inputs(fields, terrain):
    levels = jnp.arange(fields.shape[-1], dtype=jnp.int32)
    height = 2.0 * (levels - terrain[..., None]).astype(jnp.float32) / fields.shape[-1]
    return jnp.stack(
        [vertical_diff(fields[0]), vertical_diff(fields[1]), vertical_diff(fields[2]), height]
    )


def hidden_units(inputs, w_in, b_in):
    before = jnp.einsum("hf,f...->h...", w_in, inputs, precision=PRECISE)
    return jnp.tanh(before + b_in.reshape((-1,) + (1,) * (inputs.ndim - 1)))


def viscosity(hidden, w_out):
    logit = jnp.einsum("h,h...->...", w_out, hidden, precision=PRECISE)
    return 0.16 * jax.nn.sigmoid(logit)


def interior(values):
    return values[..., 1:-1, 1:-1, :]


def beside(values):
    return [
        values[..., 2:, 1:-1, :],
        values[..., :-2, 1:-1, :],
        values[..., 1:-1, 2:, :],
        values[..., 1:-1, :-2, :],
    ]


def above_below(values):
    blank = jnp.zeros_like(values[..., :1])
    return [
        jnp.concatenate([values[..., 1:], blank], axis=-1),
        jnp.concatenate([blank, values[..., :-1]], axis=-1),
    ]


def fluid_cells(terrain, levels_count):
    levels = jnp.arange(levels_count, dtype=jnp.int32)
    return (levels >= terrain[..., None]).astype(jnp.float32)


def advance(fields, viscous, fluid):
    centre = interior(fields)
    visc_mid = interior(viscous)
    fluid_mid = interior(fluid)
    near_sets = list(zip(beside(fields), beside(viscous), beside(fluid)))
    near_sets = near_sets + list(
        zip(above_below(centre), above_below(visc_mid), above_below(fluid_mid))
    )
    summed = centre
    for field_near, visc_near, fluid_near in near_sets:
        conductance = fluid_mid * fluid_near * 0.5 * (visc_mid + visc_near)
        summed = summed + conductance * (field_near - centre)
    return summed


def adjoint_step(padded, viscous, fluid, terrain, backward, w_in, b_in, w_out):
    centre = interior(padded)
    visc_mid = interior(viscous)
    fluid_mid = interior(fluid)
    back_mid = interior(backward)
    near_sets = list(zip(beside(padded), beside(viscous), beside(fluid), beside(backward)))
    near_sets = near_sets + list(
        zip(
            above_below(centre),
            above_below(visc_mid),
            above_below(fluid_mid),
            above_below(back_mid),
        )
    )
    result = back_mid
    visc_grad = jnp.zeros(visc_mid.shape, jnp.float32)
    for field_near, visc_near, fluid_near, back_near in near_sets:
        open_face = fluid_mid * fluid_near
        conductance = open_face * 0.5 * (visc_mid + visc_near)
        result = result + conductance * (back_near - back_mid)
        visc_grad = visc_grad + open_face * 0.5 * jnp.sum(
            (field_near - centre) * (back_mid - back_near), axis=0
        )
    inputs = closure_inputs(centre, terrain[1:-1, 1:-1])
    hidden = hidden_units(inputs, w_in, b_in)
    logit = jnp.einsum("h,h...->...", w_out, hidden, precision=PRECISE)
    squash = jax.nn.sigmoid(logit)
    logit_grad = visc_grad * 0.16 * squash * (1.0 - squash)
    before_grad = w_out[:, None, None, None] * logit_grad * (1.0 - hidden * hidden)
    out_grad = jnp.einsum("...,h...->h", logit_grad, hidden, precision=PRECISE)
    in_grad = jnp.einsum("h...,f...->hf", before_grad, inputs, precision=PRECISE)
    bias_grad = jnp.sum(before_grad, axis=(1, 2, 3))
    input_grad = jnp.einsum("hf,h...->f...", w_in, before_grad, precision=PRECISE)
    result = result.at[:3].add(-vertical_diff(input_grad[:3]))
    partial_grad = jnp.concatenate([in_grad, bias_grad[:, None], out_grad[:, None]], axis=1)
    return (result, partial_grad)


def seed_from(final, site_cells, site_values):
    flat = final.reshape(final.shape[0], -1)
    misfit = flat[:, site_cells] - site_values
    return jnp.zeros_like(flat).at[:, site_cells].add(misfit).reshape(final.shape)


def add_partial(grad_sum, partial_grad):
    return grad_sum + partial_grad


def body(state, terrain, site_cells, site_values, w_in, b_in, w_out):
    fields_count, width_x, width_y, levels_count = state.shape
    top_code = levels_count - terrain
    grad_sum = jnp.zeros((w_in.shape[0], w_in.shape[1] + 2), jnp.float32)
    saved = []
    code_padded = padded_2(top_code, (("gx", 0), ("gy", 1)), 1)
    terrain_padded = levels_count - code_padded
    fluid_padded = fluid_cells(terrain_padded, levels_count)
    fields = state
    for step_index in range(STEPS):
        padded = padded_2(fields, (("gx", 1), ("gy", 2)), 1)
        viscous = viscosity(hidden_units(closure_inputs(padded, terrain_padded), w_in, b_in), w_out)
        saved.append((padded, viscous, fluid_padded, terrain_padded))
        fields = advance(padded, viscous, fluid_padded)
    backward = seed_from(fields, site_cells, site_values)
    for step_index in range(STEPS - 1, -1, -1):
        padded, viscous, fluid_padded, terrain_padded = saved[step_index]
        back_padded = padded_2(backward, (("gx", 1), ("gy", 2)), 1)
        backward, partial_grad = adjoint_step(
            padded, viscous, fluid_padded, terrain_padded, back_padded, w_in, b_in, w_out
        )
        grad_sum = add_partial(grad_sum, partial_grad)
    closure_sum = lax.psum(grad_sum, ("gx", "gy"))
    site_total = site_cells.shape[0] * lax.axis_size("gx") * lax.axis_size("gy")
    return (backward, closure_sum * site_total ** (-0.5))


def solution(mesh):
    return jax.shard_map(
        body,
        mesh=mesh,
        in_specs=(
            P(None, "gx", "gy", None),
            P("gx", "gy"),
            P(("gx", "gy")),
            P(None, ("gx", "gy")),
            P(),
            P(),
            P(),
        ),
        out_specs=(P(None, "gx", "gy", None), P()),
        check_vma=False,
    )
```

profile of v0, /device:TPU:1, one launch (start us, length us, event | category | flops | bytes accessed | tf_op | source)
XLA Modules:
  0.0 348.7 jit_solution(16706777080903427037)
XLA Ops:
  1.5 4.6 %collective-permute-start.4 = (f32[5,1,8,128]{3,2,1,0:T(8,128)S(1)}, f32[5,1,8,128]{3,2,1,0:T(8,128)S(1)}, u32[]{:S(2)}, u32[]{:S(2)}) collective-permute-start(f32[5,1,8,128]{3,2,1,0:T(8,128)S(1)} %get-tuple-element.168), channel_id=1, source_target_pairs={{0,8},{8,16},{16,24},{24,32},{32,40},{40,48},{48,56},{56,64},{64,7... | collective-permute-start | bytes 61448 | tf_op jit(solution)/shard_map/ppermute | solution.py:18
  8.7 3.6 %collective-permute-start = (s32[1,8]{1,0:T(1,128)S(1)}, s32[1,8]{1,0:T(1,128)S(1)}, u32[]{:S(2)}, u32[]{:S(2)}) collective-permute-start(s32[1,8]{1,0:T(1,128)S(1)} %get-tuple-element.260), channel_id=1, source_target_pairs={{0,8},{8,16},{16,24},{24,32},{32,40},{40,48},{48,56},{56,64},{64,7... | collective-permute-start | bytes 104 | tf_op jit(solution)/shard_map/ppermute | solution.py:18
  18.9 3.1 collective-permute-start.2
  23.3 3.1 collective-permute-done.3
  26.9 3.1 collective-permute-start.6
  31.5 3.2 collective-permute-done.7
  40.9 6.5 %collective-permute-start.8 = (f32[5,1,8,128]{3,2,1,0:T(8,128)S(1)}, f32[5,1,8,128]{3,2,1,0:T(8,128)S(1)}, u32[]{:S(2)}, u32[]{:S(2)}) collective-permute-start(f32[5,1,8,128]{3,2,1,0:T(8,128)S(1)} %get-tuple-element.156), channel_id=1, source_target_pairs={{0,8},{8,16},{16,24},{24,32},{32,40},{40,48},{48,56},{56,64},{64,7... | collective-permute-start | bytes 61448 | tf_op jit(solution)/shard_map/ppermute | solution.py:18
  52.5 4.8 %collective-permute-start.10 = (f32[5,10,1,128]{3,2,1,0:T(1,128)S(1)}, f32[5,10,1,128]{3,2,1,0:T(1,128)S(1)}, u32[]{:S(2)}, u32[]{:S(2)}) collective-permute-start(f32[5,10,1,128]{3,2,1,0:T(1,128)S(1)} %get-tuple-element.114), channel_id=1, source_target_pairs={{0,1},{1,2},{2,3},{3,4},{4,5},{5,6},{6,7},{8,9},{9,10},{10,11},{11... | collective-permute-start | bytes 76808 | tf_op jit(solution)/shard_map/ppermute | solution.py:18
  58.9 3.3 collective-permute-done.11
  76.9 3.7 %collective-permute-start.14 = (f32[5,10,1,128]{3,2,1,0:T(1,128)S(1)}, f32[5,10,1,128]{3,2,1,0:T(1,128)S(1)}, u32[]{:S(2)}, u32[]{:S(2)}) collective-permute-start(f32[5,10,1,128]{3,2,1,0:T(1,128)S(1)} %get-tuple-element.112), channel_id=1, source_target_pairs={{0,1},{1,2},{2,3},{3,4},{4,5},{5,6},{6,7},{8,9},{9,10},{10,11},{11... | collective-permute-start | bytes 76808 | tf_op jit(solution)/shard_map/ppermute | solution.py:18
  82.1 3.5 collective-permute-done.15
  91.6 3.1 collective-permute-start.16
  112.6 3.7 %collective-permute-start.18 = (f32[5,10,1,128]{3,2,1,0:T(1,128)S(1)}, f32[5,10,1,128]{3,2,1,0:T(1,128)S(1)}, u32[]{:S(2)}, u32[]{:S(2)}) collective-permute-start(f32[5,10,1,128]{3,2,1,0:T(1,128)S(1)} %get-tuple-element.110), channel_id=1, source_target_pairs={{0,1},{1,2},{2,3},{3,4},{4,5},{5,6},{6,7},{8,9},{9,10},{10,11},{11... | collective-permute-start | bytes 76808 | tf_op jit(solution)/shard_map/ppermute | solution.py:18
  118.0 3.2 collective-permute-done.19
  130.5 5.8 %scatter_custom_fusion = f32[5,8192]{0,1:T(8,128)} fusion(s32[256]{0:T(256)} %copy-done.109, f32[]{:T(128)} %constant.113.clone.1, f32[5,256]{0,1:T(8,128)} %copy.50, f32[5,8192]{0,1:T(8,128)} %bitcast.362, s32[1024]{0:T(1024)S(1)} %pad_clamp_fusion), kind=kCustom, calls=%fused_computation.50 | custom fusion | flops 2560 | bytes 4493824 | tf_op jit(solution)/shard_map/scatter-add | solution.py:134
  141.3 4.8 %collective-permute-start.21 = (f32[5,1,8,128]{3,2,1,0:T(8,128)S(1)}, f32[5,1,8,128]{3,2,1,0:T(8,128)S(1)}, u32[]{:S(2)}, u32[]{:S(2)}) collective-permute-start(f32[5,1,8,128]{3,2,1,0:T(8,128)S(1)} %get-tuple-element.144), channel_id=1, source_target_pairs={{0,8},{8,16},{16,24},{24,32},{32,40},{40,48},{48,56},{56,64},{64,7... | collective-permute-start | bytes 61448 | tf_op jit(solution)/shard_map/ppermute | solution.py:18
  148.4 4.6 %collective-permute-start.23 = (f32[5,10,1,128]{3,2,1,0:T(1,128)S(1)}, f32[5,10,1,128]{3,2,1,0:T(1,128)S(1)}, u32[]{:S(2)}, u32[]{:S(2)}) collective-permute-start(f32[5,10,1,128]{3,2,1,0:T(1,128)S(1)} %get-tuple-element.109), channel_id=1, source_target_pairs={{0,1},{1,2},{2,3},{3,4},{4,5},{5,6},{6,7},{8,9},{9,10},{10,11},{11... | collective-permute-start | bytes 76808 | tf_op jit(solution)/shard_map/ppermute | solution.py:18
  161.0 6.4 %collective-permute-start.25 = (f32[5,1,8,128]{3,2,1,0:T(8,128)S(1)}, f32[5,1,8,128]{3,2,1,0:T(8,128)S(1)}, u32[]{:S(2)}, u32[]{:S(2)}) collective-permute-start(f32[5,1,8,128]{3,2,1,0:T(8,128)S(1)} %get-tuple-element.137), channel_id=1, source_target_pairs={{0,8},{8,16},{16,24},{24,32},{32,40},{40,48},{48,56},{56,64},{64,7... | collective-permute-start | bytes 61448 | tf_op jit(solution)/shard_map/ppermute | solution.py:18
  170.5 4.6 %collective-permute-start.27 = (f32[5,10,1,128]{3,2,1,0:T(1,128)S(1)}, f32[5,10,1,128]{3,2,1,0:T(1,128)S(1)}, u32[]{:S(2)}, u32[]{:S(2)}) collective-permute-start(f32[5,10,1,128]{3,2,1,0:T(1,128)S(1)} %get-tuple-element.107), channel_id=1, source_target_pairs={{0,1},{1,2},{2,3},{3,4},{4,5},{5,6},{6,7},{8,9},{9,10},{10,11},{11... | collective-permute-start | bytes 76808 | tf_op jit(solution)/shard_map/ppermute | solution.py:18
  182.8 7.3 %collective-permute-start.29 = (f32[5,1,8,128]{3,2,1,0:T(8,128)S(1)}, f32[5,1,8,128]{3,2,1,0:T(8,128)S(1)}, u32[]{:S(2)}, u32[]{:S(2)}) collective-permute-start(f32[5,1,8,128]{3,2,1,0:T(8,128)S(1)} %get-tuple-element.130), channel_id=1, source_target_pairs={{0,8},{8,16},{16,24},{24,32},{32,40},{40,48},{48,56},{56,64},{64,7... | collective-permute-start | bytes 61448 | tf_op jit(solution)/shard_map/ppermute | solution.py:18
  193.3 4.8 %collective-permute-start.31 = (f32[5,10,1,128]{3,2,1,0:T(1,128)S(1)}, f32[5,10,1,128]{3,2,1,0:T(1,128)S(1)}, u32[]{:S(2)}, u32[]{:S(2)}) collective-permute-start(f32[5,10,1,128]{3,2,1,0:T(1,128)S(1)} %get-tuple-element.105), channel_id=1, source_target_pairs={{0,1},{1,2},{2,3},{3,4},{4,5},{5,6},{6,7},{8,9},{9,10},{10,11},{11... | collective-permute-start | bytes 76808 | tf_op jit(solution)/shard_map/ppermute | solution.py:18
  205.6 4.5 %collective-permute-start.33 = (f32[5,1,8,128]{3,2,1,0:T(8,128)S(1)}, f32[5,1,8,128]{3,2,1,0:T(8,128)S(1)}, u32[]{:S(2)}, u32[]{:S(2)}) collective-permute-start(f32[5,1,8,128]{3,2,1,0:T(8,128)S(1)} %get-tuple-element.123), channel_id=1, source_target_pairs={{0,8},{8,16},{16,24},{24,32},{32,40},{40,48},{48,56},{56,64},{64,7... | collective-permute-start | bytes 61448 | tf_op jit(solution)/shard_map/ppermute | solution.py:18
  213.2 6.2 %collective-permute-start.35 = (f32[5,10,1,128]{3,2,1,0:T(1,128)S(1)}, f32[5,10,1,128]{3,2,1,0:T(1,128)S(1)}, u32[]{:S(2)}, u32[]{:S(2)}) collective-permute-start(f32[5,10,1,128]{3,2,1,0:T(1,128)S(1)} %get-tuple-element.103), channel_id=1, source_target_pairs={{0,1},{1,2},{2,3},{3,4},{4,5},{5,6},{6,7},{8,9},{9,10},{10,11},{11... | collective-permute-start | bytes 76808 | tf_op jit(solution)/shard_map/ppermute | solution.py:18
  227.6 118.9 %psum.7 = f32[64,6]{0,1:T(8,128)S(1)} all-reduce(f32[64,6]{0,1:T(8,128)S(1)} %fusion.281), channel_id=1, replica_groups=mesh['gx'=32,'gy'=8] {'gx','gy'}, use_global_device_ids=true, to_apply=%region_29.0 | all-reduce | flops 384 | bytes 3072 | tf_op jit(solution)/shard_map/psum | solution.py:163
  (447 shorter events, 124.7 us)
Async XLA Ops:
  1.5 25.4 %collective-permute-start.4 = (f32[5,1,8,128]{3,2,1,0:T(8,128)S(1)}, f32[5,1,8,128]{3,2,1,0:T(8,128)S(1)}, u32[]{:S(2)}, u32[]{:S(2)}) collective-permute-start(f32[5,1,8,128]{3,2,1,0:T(8,128)S(1)} %get-tuple-element.168), channel_id=1, source_target_pairs={{0,8},{8,16},{16,24},{24,32},{32,40},{40,48},{48,56},{56,64},{64,7... | collective-permute-start | bytes 61448 | tf_op jit(solution)/shard_map/ppermute | solution.py:18
  6.0 20.8 %collective-permute-start.5 = (f32[5,1,8,128]{3,2,1,0:T(8,128)S(1)}, f32[5,1,8,128]{3,2,1,0:T(8,128)S(1)}, u32[]{:S(2)}, u32[]{:S(2)}) collective-permute-start(f32[5,1,8,128]{3,2,1,0:T(8,128)S(1)} %get-tuple-element.169), channel_id=1, source_target_pairs={{8,0},{16,8},{24,16},{32,24},{40,32},{48,40},{56,48},{64,56},{72,6... | collective-permute-start | bytes 61448 | tf_op jit(solution)/shard_map/ppermute | solution.py:20
  8.7 10.1 %collective-permute-start = (s32[1,8]{1,0:T(1,128)S(1)}, s32[1,8]{1,0:T(1,128)S(1)}, u32[]{:S(2)}, u32[]{:S(2)}) collective-permute-start(s32[1,8]{1,0:T(1,128)S(1)} %get-tuple-element.260), channel_id=1, source_target_pairs={{0,8},{8,16},{16,24},{24,32},{32,40},{40,48},{48,56},{56,64},{64,7... | collective-permute-start | bytes 104 | tf_op jit(solution)/shard_map/ppermute | solution.py:18
  12.3 6.5 %collective-permute-start.1 = (s32[1,8]{1,0:T(1,128)S(1)}, s32[1,8]{1,0:T(1,128)S(1)}, u32[]{:S(2)}, u32[]{:S(2)}) collective-permute-start(s32[1,8]{1,0:T(1,128)S(1)} %get-tuple-element.261), channel_id=1, source_target_pairs={{8,0},{16,8},{24,16},{32,24},{40,32},{48,40},{56,48},{64,56},{72,6... | collective-permute-start | bytes 104 | tf_op jit(solution)/shard_map/ppermute | solution.py:20
  40.9 8.8 %collective-permute-start.8 = (f32[5,1,8,128]{3,2,1,0:T(8,128)S(1)}, f32[5,1,8,128]{3,2,1,0:T(8,128)S(1)}, u32[]{:S(2)}, u32[]{:S(2)}) collective-permute-start(f32[5,1,8,128]{3,2,1,0:T(8,128)S(1)} %get-tuple-element.156), channel_id=1, source_target_pairs={{0,8},{8,16},{16,24},{24,32},{32,40},{40,48},{48,56},{56,64},{64,7... | collective-permute-start | bytes 61448 | tf_op jit(solution)/shard_map/ppermute | solution.py:18
  52.5 6.4 %collective-permute-start.10 = (f32[5,10,1,128]{3,2,1,0:T(1,128)S(1)}, f32[5,10,1,128]{3,2,1,0:T(1,128)S(1)}, u32[]{:S(2)}, u32[]{:S(2)}) collective-permute-start(f32[5,10,1,128]{3,2,1,0:T(1,128)S(1)} %get-tuple-element.114), channel_id=1, source_target_pairs={{0,1},{1,2},{2,3},{3,4},{4,5},{5,6},{6,7},{8,9},{9,10},{10,11},{11... | collective-permute-start | bytes 76808 | tf_op jit(solution)/shard_map/ppermute | solution.py:18
  91.6 20.9 %collective-permute-start.16 = (f32[5,1,8,128]{3,2,1,0:T(8,128)S(1)}, f32[5,1,8,128]{3,2,1,0:T(8,128)S(1)}, u32[]{:S(2)}, u32[]{:S(2)}) collective-permute-start(f32[5,1,8,128]{3,2,1,0:T(8,128)S(1)} %get-tuple-element.148), channel_id=1, source_target_pairs={{0,8},{8,16},{16,24},{24,32},{32,40},{40,48},{48,56},{56,64},{64,7... | collective-permute-start | bytes 61448 | tf_op jit(solution)/shard_map/ppermute | solution.py:18
  94.7 17.9 %collective-permute-start.17 = (f32[5,1,8,128]{3,2,1,0:T(8,128)S(1)}, f32[5,1,8,128]{3,2,1,0:T(8,128)S(1)}, u32[]{:S(2)}, u32[]{:S(2)}) collective-permute-start(f32[5,1,8,128]{3,2,1,0:T(8,128)S(1)} %get-tuple-element.149), channel_id=1, source_target_pairs={{8,0},{16,8},{24,16},{32,24},{40,32},{48,40},{56,48},{64,56},{72,6... | collective-permute-start | bytes 61448 | tf_op jit(solution)/shard_map/ppermute | solution.py:20
  139.3 7.0 %collective-permute-start.20 = (f32[5,1,8,128]{3,2,1,0:T(8,128)S(1)}, f32[5,1,8,128]{3,2,1,0:T(8,128)S(1)}, u32[]{:S(2)}, u32[]{:S(2)}) collective-permute-start(f32[5,1,8,128]{3,2,1,0:T(8,128)S(1)} %get-tuple-element.145), channel_id=1, source_target_pairs={{8,0},{16,8},{24,16},{32,24},{40,32},{48,40},{56,48},{64,56},{72,6... | collective-permute-start | bytes 61448 | tf_op jit(solution)/shard_map/ppermute | solution.py:20
  141.3 5.7 %collective-permute-start.21 = (f32[5,1,8,128]{3,2,1,0:T(8,128)S(1)}, f32[5,1,8,128]{3,2,1,0:T(8,128)S(1)}, u32[]{:S(2)}, u32[]{:S(2)}) collective-permute-start(f32[5,1,8,128]{3,2,1,0:T(8,128)S(1)} %get-tuple-element.144), channel_id=1, source_target_pairs={{0,8},{8,16},{16,24},{24,32},{32,40},{40,48},{48,56},{56,64},{64,7... | collective-permute-start | bytes 61448 | tf_op jit(solution)/shard_map/ppermute | solution.py:18
  147.1 7.1 %collective-permute-start.22 = (f32[5,10,1,128]{3,2,1,0:T(1,128)S(1)}, f32[5,10,1,128]{3,2,1,0:T(1,128)S(1)}, u32[]{:S(2)}, u32[]{:S(2)}) collective-permute-start(f32[5,10,1,128]{3,2,1,0:T(1,128)S(1)} %get-tuple-element.108), channel_id=1, source_target_pairs={{1,0},{2,1},{3,2},{4,3},{5,4},{6,5},{7,6},{9,8},{10,9},{11,10},{12... | collective-permute-start | bytes 76808 | tf_op jit(solution)/shard_map/ppermute | solution.py:20
  148.4 5.8 %collective-permute-start.23 = (f32[5,10,1,128]{3,2,1,0:T(1,128)S(1)}, f32[5,10,1,128]{3,2,1,0:T(1,128)S(1)}, u32[]{:S(2)}, u32[]{:S(2)}) collective-permute-start(f32[5,10,1,128]{3,2,1,0:T(1,128)S(1)} %get-tuple-element.109), channel_id=1, source_target_pairs={{0,1},{1,2},{2,3},{3,4},{4,5},{5,6},{6,7},{8,9},{9,10},{10,11},{11... | collective-permute-start | bytes 76808 | tf_op jit(solution)/shard_map/ppermute | solution.py:18
  159.0 10.2 %collective-permute-start.24 = (f32[5,1,8,128]{3,2,1,0:T(8,128)S(1)}, f32[5,1,8,128]{3,2,1,0:T(8,128)S(1)}, u32[]{:S(2)}, u32[]{:S(2)}) collective-permute-start(f32[5,1,8,128]{3,2,1,0:T(8,128)S(1)} %get-tuple-element.138), channel_id=1, source_target_pairs={{8,0},{16,8},{24,16},{32,24},{40,32},{48,40},{56,48},{64,56},{72,6... | collective-permute-start | bytes 61448 | tf_op jit(solution)/shard_map/ppermute | solution.py:20
  161.0 8.1 %collective-permute-start.25 = (f32[5,1,8,128]{3,2,1,0:T(8,128)S(1)}, f32[5,1,8,128]{3,2,1,0:T(8,128)S(1)}, u32[]{:S(2)}, u32[]{:S(2)}) collective-permute-start(f32[5,1,8,128]{3,2,1,0:T(8,128)S(1)} %get-tuple-element.137), channel_id=1, source_target_pairs={{0,8},{8,16},{16,24},{24,32},{32,40},{40,48},{48,56},{56,64},{64,7... | collective-permute-start | bytes 61448 | tf_op jit(solution)/shard_map/ppermute | solution.py:18
  169.2 6.1 %collective-permute-start.26 = (f32[5,10,1,128]{3,2,1,0:T(1,128)S(1)}, f32[5,10,1,128]{3,2,1,0:T(1,128)S(1)}, u32[]{:S(2)}, u32[]{:S(2)}) collective-permute-start(f32[5,10,1,128]{3,2,1,0:T(1,128)S(1)} %get-tuple-element.106), channel_id=1, source_target_pairs={{1,0},{2,1},{3,2},{4,3},{5,4},{6,5},{7,6},{9,8},{10,9},{11,10},{12... | collective-permute-start | bytes 76808 | tf_op jit(solution)/shard_map/ppermute | solution.py:20
  170.5 5.5 %collective-permute-start.27 = (f32[5,10,1,128]{3,2,1,0:T(1,128)S(1)}, f32[5,10,1,128]{3,2,1,0:T(1,128)S(1)}, u32[]{:S(2)}, u32[]{:S(2)}) collective-permute-start(f32[5,10,1,128]{3,2,1,0:T(1,128)S(1)} %get-tuple-element.107), channel_id=1, source_target_pairs={{0,1},{1,2},{2,3},{3,4},{4,5},{5,6},{6,7},{8,9},{9,10},{10,11},{11... | collective-permute-start | bytes 76808 | tf_op jit(solution)/shard_map/ppermute | solution.py:18
  180.8 11.2 %collective-permute-start.28 = (f32[5,1,8,128]{3,2,1,0:T(8,128)S(1)}, f32[5,1,8,128]{3,2,1,0:T(8,128)S(1)}, u32[]{:S(2)}, u32[]{:S(2)}) collective-permute-start(f32[5,1,8,128]{3,2,1,0:T(8,128)S(1)} %get-tuple-element.131), channel_id=1, source_target_pairs={{8,0},{16,8},{24,16},{32,24},{40,32},{48,40},{56,48},{64,56},{72,6... | collective-permute-start | bytes 61448 | tf_op jit(solution)/shard_map/ppermute | solution.py:20
  182.8 9.1 %collective-permute-start.29 = (f32[5,1,8,128]{3,2,1,0:T(8,128)S(1)}, f32[5,1,8,128]{3,2,1,0:T(8,128)S(1)}, u32[]{:S(2)}, u32[]{:S(2)}) collective-permute-start(f32[5,1,8,128]{3,2,1,0:T(8,128)S(1)} %get-tuple-element.130), channel_id=1, source_target_pairs={{0,8},{8,16},{16,24},{24,32},{32,40},{40,48},{48,56},{56,64},{64,7... | collective-permute-start | bytes 61448 | tf_op jit(solution)/shard_map/ppermute | solution.py:18
  192.0 6.3 %collective-permute-start.30 = (f32[5,10,1,128]{3,2,1,0:T(1,128)S(1)}, f32[5,10,1,128]{3,2,1,0:T(1,128)S(1)}, u32[]{:S(2)}, u32[]{:S(2)}) collective-permute-start(f32[5,10,1,128]{3,2,1,0:T(1,128)S(1)} %get-tuple-element.104), channel_id=1, source_target_pairs={{1,0},{2,1},{3,2},{4,3},{5,4},{6,5},{7,6},{9,8},{10,9},{11,10},{12... | collective-permute-start | bytes 76808 | tf_op jit(solution)/shard_map/ppermute | solution.py:20
  193.3 5.5 %collective-permute-start.31 = (f32[5,10,1,128]{3,2,1,0:T(1,128)S(1)}, f32[5,10,1,128]{3,2,1,0:T(1,128)S(1)}, u32[]{:S(2)}, u32[]{:S(2)}) collective-permute-start(f32[5,10,1,128]{3,2,1,0:T(1,128)S(1)} %get-tuple-element.105), channel_id=1, source_target_pairs={{0,1},{1,2},{2,3},{3,4},{4,5},{5,6},{6,7},{8,9},{9,10},{10,11},{11... | collective-permute-start | bytes 76808 | tf_op jit(solution)/shard_map/ppermute | solution.py:18
  203.5 8.4 %collective-permute-start.32 = (f32[5,1,8,128]{3,2,1,0:T(8,128)S(1)}, f32[5,1,8,128]{3,2,1,0:T(8,128)S(1)}, u32[]{:S(2)}, u32[]{:S(2)}) collective-permute-start(f32[5,1,8,128]{3,2,1,0:T(8,128)S(1)} %get-tuple-element.124), channel_id=1, source_target_pairs={{8,0},{16,8},{24,16},{32,24},{40,32},{48,40},{56,48},{64,56},{72,6... | collective-permute-start | bytes 61448 | tf_op jit(solution)/shard_map/ppermute | solution.py:20
  205.6 6.3 %collective-permute-start.33 = (f32[5,1,8,128]{3,2,1,0:T(8,128)S(1)}, f32[5,1,8,128]{3,2,1,0:T(8,128)S(1)}, u32[]{:S(2)}, u32[]{:S(2)}) collective-permute-start(f32[5,1,8,128]{3,2,1,0:T(8,128)S(1)} %get-tuple-element.123), channel_id=1, source_target_pairs={{0,8},{8,16},{16,24},{24,32},{32,40},{40,48},{48,56},{56,64},{64,7... | collective-permute-start | bytes 61448 | tf_op jit(solution)/shard_map/ppermute | solution.py:18
  211.9 7.7 %collective-permute-start.34 = (f32[5,10,1,128]{3,2,1,0:T(1,128)S(1)}, f32[5,10,1,128]{3,2,1,0:T(1,128)S(1)}, u32[]{:S(2)}, u32[]{:S(2)}) collective-permute-start(f32[5,10,1,128]{3,2,1,0:T(1,128)S(1)} %get-tuple-element.102), channel_id=1, source_target_pairs={{1,0},{2,1},{3,2},{4,3},{5,4},{6,5},{7,6},{9,8},{10,9},{11,10},{12... | collective-permute-start | bytes 76808 | tf_op jit(solution)/shard_map/ppermute | solution.py:20
  213.2 7.2 %collective-permute-start.35 = (f32[5,10,1,128]{3,2,1,0:T(1,128)S(1)}, f32[5,10,1,128]{3,2,1,0:T(1,128)S(1)}, u32[]{:S(2)}, u32[]{:S(2)}) collective-permute-start(f32[5,10,1,128]{3,2,1,0:T(1,128)S(1)} %get-tuple-element.103), channel_id=1, source_target_pairs={{0,1},{1,2},{2,3},{3,4},{4,5},{5,6},{6,7},{8,9},{9,10},{10,11},{11... | collective-permute-start | bytes 76808 | tf_op jit(solution)/shard_map/ppermute | solution.py:18
  (122 other events, 1801.3 us)
where the time goes:
time: 356 us; the launch traced here: 349 us
  blocking collectives  119 us (33%)
  starting transfers between devices  113 us (32%)
  matrix products  55.2 us (16%)
  waiting for transfers between devices  24.6 us (7%)
  other arithmetic  17.4 us (5%)
  local copies, waits for them, and re-layouts  16.3 us (5%)
    psum x1, blocking collectives, body(): closure_sum = lax.psum(grad_sum, ('gx', 'gy'))  119 us
    ppermute x18, starting transfers between devices, padded_2(): lax.ppermute(tail, axis, [(i, (i + 1) % count) for i in range(ends)])  82.5 us
    ppermute x18, starting transfers between devices, padded_2(): lax.ppermute(head, axis, [((i + 1) % count, i) for i in range(ends)])  30.2 us
    ppermute x18, waiting for transfers between devices, padded_2(): lax.ppermute(head, axis, [((i + 1) % count, i) for i in range(ends)])  21.8 us
    dot_general x8, matrix products, hidden_units(): before = jnp.einsum('hf,f...->h...', w_in, inputs, precision=PRECISE)  18.7 us
    dot_general x4, matrix products, viscosity(): logit = jnp.einsum('h,h...->...', w_out, hidden, precision=PRECISE)  8.33 us
    dot_general x4, matrix products, adjoint_step(): jnp.einsum('h...,f...->hf', before_grad, inputs, precision=PRECISE)  7.91 us
    dot_general x4, matrix products, adjoint_step(): logit = jnp.einsum('h,h...->...', w_out, hidden, precision=PRECISE)  7.21 us
  transfers between devices with their start and end apart: 36, of which 11 were waited for; matrix products, arithmetic and copies ran while one was open for 8% of the time, Pallas kernels for 0%

commit v1 on v0

--- a/solution.py
+++ b/solution.py
@@ -160,7 +160,7 @@
             padded, viscous, fluid_padded, terrain_padded, back_padded, w_in, b_in, w_out
         )
         grad_sum = add_partial(grad_sum, partial_grad)
-    closure_sum = lax.psum(grad_sum, ("gx", "gy"))
+    closure_sum = jnp.sum(lax.all_gather(grad_sum, ("gx", "gy")), axis=0)
     site_total = site_cells.shape[0] * lax.axis_size("gx") * lax.axis_size("gy")
     return (backward, closure_sum * site_total ** (-0.5))
 

time: 356 us -> 902 us (2.53)
  the two profiles are of different devices: /device:TPU:1 before, /device:TPU:128 now
where the time goes in v1:
time: 902 us; the launch traced here: 895 us
  blocking collectives  634 us (70%)
  starting transfers between devices  119 us (13%)
  matrix products  55.1 us (6%)
  waiting for transfers between devices  49.3 us (5%)
  other arithmetic  17.7 us (2%)
  local copies, waits for them, and re-layouts  16.7 us (2%)
    all_gather x1, blocking collectives, body(): closure_sum = jnp.sum(lax.all_gather(grad_sum, ('gx', 'gy')), axis=0)  634 us
    ppermute x18, starting transfers between devices, padded_2(): lax.ppermute(head, axis, [((i + 1) % count, i) for i in range(ends)])  59.9 us
    ppermute x18, starting transfers between devices, padded_2(): lax.ppermute(tail, axis, [(i, (i + 1) % count) for i in range(ends)])  59.2 us
    ppermute x18, waiting for transfers between devices, padded_2(): lax.ppermute(tail, axis, [(i, (i + 1) % count) for i in range(ends)])  26.3 us
    ppermute x18, waiting for transfers between devices, padded_2(): lax.ppermute(head, axis, [((i + 1) % count, i) for i in range(ends)])  23 us
    dot_general x8, matrix products, hidden_units(): before = jnp.einsum('hf,f...->h...', w_in, inputs, precision=PRECISE)  18.7 us
  transfers between devices with their start and end apart: 36, of which 17 were waited for; matrix products, arithmetic and copies ran while one was open for 3% of the time, Pallas kernels for 0%

profile of v1, /device:TPU:128, one launch (start us, length us, event | category | flops | bytes accessed | tf_op | source)
XLA Modules:
  0.0 895.2 jit_solution(306906273524392911)
XLA Ops:
  3.4 7.9 collective-permute-start.5
  13.9 7.9 collective-permute-start.1
  31.1 4.2 collective-permute-done.3
  36.0 3.4 collective-permute-start.6
  40.9 4.2 collective-permute-done.7
  53.4 7.9 collective-permute-start.9
  62.7 4.1 collective-permute-start.10
  68.5 4.1 collective-permute-done.11
  81.1 7.9 collective-permute-start.13
  90.5 4.0 collective-permute-start.14
  96.1 4.2 collective-permute-done.15
  108.2 8.3 collective-permute-start.17
  132.1 4.0 collective-permute-start.18
  137.7 4.1 collective-permute-done.19
  151.3 5.8 scatter_custom_fusion
  164.6 6.8 collective-permute-done.21
  172.8 4.9 collective-permute-start.23
  189.9 5.2 collective-permute-done.25
  196.4 4.8 collective-permute-start.27
  213.7 5.2 collective-permute-done.29
  220.2 5.1 collective-permute-start.31
  237.5 5.2 collective-permute-done.33
  244.0 6.2 collective-permute-start.35
  259.0 633.8 %all_gather.4 = f32[256,64,6]{1,2,0:T(8,128)S(1)} all-gather(f32[1,64,6]{1,2,0:T(8,128)S(1)} %fusion.289), channel_id=1, replica_groups=mesh['gx'=32,'gy'=8] {'gx','gy'}, dimensions={0}, use_global_device_ids=true | all-gather | bytes 394752 | tf_op jit(solution)/shard_map/all_gather | solution.py:163
  (453 shorter events, 132.7 us)
Async XLA Ops:
  1.5 34.4 %collective-permute-start.4 = (f32[5,1,8,128]{3,2,1,0:T(8,128)S(1)}, f32[5,1,8,128]{3,2,1,0:T(8,128)S(1)}, u32[]{:S(2)}, u32[]{:S(2)}) collective-permute-start(f32[5,1,8,128]{3,2,1,0:T(8,128)S(1)} %get-tuple-element.168), channel_id=1, source_target_pairs={{0,8},{8,16},{16,24},{24,32},{32,40},{40,48},{48,56},{56,64},{64,7... | collective-permute-start | bytes 61448 | tf_op jit(solution)/shard_map/ppermute | solution.py:18
  3.4 32.5 %collective-permute-start.5 = (f32[5,1,8,128]{3,2,1,0:T(8,128)S(1)}, f32[5,1,8,128]{3,2,1,0:T(8,128)S(1)}, u32[]{:S(2)}, u32[]{:S(2)}) collective-permute-start(f32[5,1,8,128]{3,2,1,0:T(8,128)S(1)} %get-tuple-element.169), channel_id=1, source_target_pairs={{8,0},{16,8},{24,16},{32,24},{40,32},{48,40},{56,48},{64,56},{72,6... | collective-permute-start | bytes 61448 | tf_op jit(solution)/shard_map/ppermute | solution.py:20
  11.9 14.4 %collective-permute-start = (s32[1,8]{1,0:T(1,128)S(1)}, s32[1,8]{1,0:T(1,128)S(1)}, u32[]{:S(2)}, u32[]{:S(2)}) collective-permute-start(s32[1,8]{1,0:T(1,128)S(1)} %get-tuple-element.260), channel_id=1, source_target_pairs={{0,8},{8,16},{16,24},{24,32},{32,40},{40,48},{48,56},{56,64},{64,7... | collective-permute-start | bytes 104 | tf_op jit(solution)/shard_map/ppermute | solution.py:18
  13.9 12.4 %collective-permute-start.1 = (s32[1,8]{1,0:T(1,128)S(1)}, s32[1,8]{1,0:T(1,128)S(1)}, u32[]{:S(2)}, u32[]{:S(2)}) collective-permute-start(s32[1,8]{1,0:T(1,128)S(1)} %get-tuple-element.261), channel_id=1, source_target_pairs={{8,0},{16,8},{24,16},{32,24},{40,32},{48,40},{56,48},{64,56},{72,6... | collective-permute-start | bytes 104 | tf_op jit(solution)/shard_map/ppermute | solution.py:20
  51.4 10.2 %collective-permute-start.8 = (f32[5,1,8,128]{3,2,1,0:T(8,128)S(1)}, f32[5,1,8,128]{3,2,1,0:T(8,128)S(1)}, u32[]{:S(2)}, u32[]{:S(2)}) collective-permute-start(f32[5,1,8,128]{3,2,1,0:T(8,128)S(1)} %get-tuple-element.156), channel_id=1, source_target_pairs={{0,8},{8,16},{16,24},{24,32},{32,40},{40,48},{48,56},{56,64},{64,7... | collective-permute-start | bytes 61448 | tf_op jit(solution)/shard_map/ppermute | solution.py:18
  53.4 9.3 %collective-permute-start.9 = (f32[5,1,8,128]{3,2,1,0:T(8,128)S(1)}, f32[5,1,8,128]{3,2,1,0:T(8,128)S(1)}, u32[]{:S(2)}, u32[]{:S(2)}) collective-permute-start(f32[5,1,8,128]{3,2,1,0:T(8,128)S(1)} %get-tuple-element.157), channel_id=1, source_target_pairs={{8,0},{16,8},{24,16},{32,24},{40,32},{48,40},{56,48},{64,56},{72,6... | collective-permute-start | bytes 61448 | tf_op jit(solution)/shard_map/ppermute | solution.py:20
  79.2 10.2 %collective-permute-start.12 = (f32[5,1,8,128]{3,2,1,0:T(8,128)S(1)}, f32[5,1,8,128]{3,2,1,0:T(8,128)S(1)}, u32[]{:S(2)}, u32[]{:S(2)}) collective-permute-start(f32[5,1,8,128]{3,2,1,0:T(8,128)S(1)} %get-tuple-element.152), channel_id=1, source_target_pairs={{0,8},{8,16},{16,24},{24,32},{32,40},{40,48},{48,56},{56,64},{64,7... | collective-permute-start | bytes 61448 | tf_op jit(solution)/shard_map/ppermute | solution.py:18
  81.1 9.3 %collective-permute-start.13 = (f32[5,1,8,128]{3,2,1,0:T(8,128)S(1)}, f32[5,1,8,128]{3,2,1,0:T(8,128)S(1)}, u32[]{:S(2)}, u32[]{:S(2)}) collective-permute-start(f32[5,1,8,128]{3,2,1,0:T(8,128)S(1)} %get-tuple-element.153), channel_id=1, source_target_pairs={{8,0},{16,8},{24,16},{32,24},{40,32},{48,40},{56,48},{64,56},{72,6... | collective-permute-start | bytes 61448 | tf_op jit(solution)/shard_map/ppermute | solution.py:20
  106.3 25.7 %collective-permute-start.16 = (f32[5,1,8,128]{3,2,1,0:T(8,128)S(1)}, f32[5,1,8,128]{3,2,1,0:T(8,128)S(1)}, u32[]{:S(2)}, u32[]{:S(2)}) collective-permute-start(f32[5,1,8,128]{3,2,1,0:T(8,128)S(1)} %get-tuple-element.148), channel_id=1, source_target_pairs={{0,8},{8,16},{16,24},{24,32},{32,40},{40,48},{48,56},{56,64},{64,7... | collective-permute-start | bytes 61448 | tf_op jit(solution)/shard_map/ppermute | solution.py:18
  108.2 23.8 %collective-permute-start.17 = (f32[5,1,8,128]{3,2,1,0:T(8,128)S(1)}, f32[5,1,8,128]{3,2,1,0:T(8,128)S(1)}, u32[]{:S(2)}, u32[]{:S(2)}) collective-permute-start(f32[5,1,8,128]{3,2,1,0:T(8,128)S(1)} %get-tuple-element.149), channel_id=1, source_target_pairs={{8,0},{16,8},{24,16},{32,24},{40,32},{48,40},{56,48},{64,56},{72,6... | collective-permute-start | bytes 61448 | tf_op jit(solution)/shard_map/ppermute | solution.py:20
  162.1 9.3 %collective-permute-start.21 = (f32[5,1,8,128]{3,2,1,0:T(8,128)S(1)}, f32[5,1,8,128]{3,2,1,0:T(8,128)S(1)}, u32[]{:S(2)}, u32[]{:S(2)}) collective-permute-start(f32[5,1,8,128]{3,2,1,0:T(8,128)S(1)} %get-tuple-element.144), channel_id=1, source_target_pairs={{0,8},{8,16},{16,24},{24,32},{32,40},{40,48},{48,56},{56,64},{64,7... | collective-permute-start | bytes 61448 | tf_op jit(solution)/shard_map/ppermute | solution.py:18
  171.5 7.4 collective-permute-start.22
  183.7 6.2 collective-permute-start.24
  185.8 9.3 %collective-permute-start.25 = (f32[5,1,8,128]{3,2,1,0:T(8,128)S(1)}, f32[5,1,8,128]{3,2,1,0:T(8,128)S(1)}, u32[]{:S(2)}, u32[]{:S(2)}) collective-permute-start(f32[5,1,8,128]{3,2,1,0:T(8,128)S(1)} %get-tuple-element.137), channel_id=1, source_target_pairs={{0,8},{8,16},{16,24},{24,32},{32,40},{40,48},{48,56},{56,64},{64,7... | collective-permute-start | bytes 61448 | tf_op jit(solution)/shard_map/ppermute | solution.py:18
  195.1 6.4 collective-permute-start.26
  196.4 6.4 collective-permute-start.27
  207.5 6.2 collective-permute-start.28
  209.6 9.3 %collective-permute-start.29 = (f32[5,1,8,128]{3,2,1,0:T(8,128)S(1)}, f32[5,1,8,128]{3,2,1,0:T(8,128)S(1)}, u32[]{:S(2)}, u32[]{:S(2)}) collective-permute-start(f32[5,1,8,128]{3,2,1,0:T(8,128)S(1)} %get-tuple-element.130), channel_id=1, source_target_pairs={{0,8},{8,16},{16,24},{24,32},{32,40},{40,48},{48,56},{56,64},{64,7... | collective-permute-start | bytes 61448 | tf_op jit(solution)/shard_map/ppermute | solution.py:18
  218.9 6.6 collective-permute-start.30
  220.2 6.4 collective-permute-start.31
  231.3 6.2 collective-permute-start.32
  233.4 9.3 %collective-permute-start.33 = (f32[5,1,8,128]{3,2,1,0:T(8,128)S(1)}, f32[5,1,8,128]{3,2,1,0:T(8,128)S(1)}, u32[]{:S(2)}, u32[]{:S(2)}) collective-permute-start(f32[5,1,8,128]{3,2,1,0:T(8,128)S(1)} %get-tuple-element.123), channel_id=1, source_target_pairs={{0,8},{8,16},{16,24},{24,32},{32,40},{40,48},{48,56},{56,64},{64,7... | collective-permute-start | bytes 61448 | tf_op jit(solution)/shard_map/ppermute | solution.py:18
  242.7 7.7 collective-permute-start.34
  244.0 7.7 collective-permute-start.35
  (122 other events, 5050.0 us)
